TPU v7x, 256 devices: a whole 4x4x8 slice. The times are simulated.
256 devices in a mesh: row: 16 (over y, x), col: 16 (over z, core).
Axes of the slice: x: 4, y: 4, z: 8, core: 2. Of those that a mesh axis runs over, the one named last changes fastest.
Arguments:
- q_seq: bfloat16 [2048, 6144], P('row', 'col'), may hold values from -4.5 to 4.5
- k_seq: bfloat16 [2048, 6144], P('row', 'col'), may hold values from -4.5 to 4.5
- v_seq: bfloat16 [2048, 6144], P('row', 'col'), may hold values from -6 to 6
- resid: bfloat16 [2048, 6144], P('row', 'col'), may hold values from -90 to 90
- ln_gain: float32 [6144], replicated, may hold values from 0.1 to 1.9
- w_up: bfloat16 [6144, 24576], P('row', 'col'), may hold values from -0.078125 to 0.078125
Outputs:
- hidden: bfloat16 [2048, 24576], P('row', 'col')
All inputs are finite; a program needn't handle non-finite values.
Results may differ from a plain program's by a relative error of at most 0.0051.
Values may be sent and summed in bfloat16 or wider, within the bound.
No kernel may reach another device: no remote copies, remote signals or barrier semaphores. Data moves between devices by JAX's collectives and lax.ppermute only.
A program may use at most 64 MiB of HBM per device.

v0:
```python
import math
import jax
import jax.numpy as jnp
from jax import lax
from jax.sharding import PartitionSpec as P

HD = 128


def attention_block(query, keys, values):
    seq, width = query.shape
    heads = width // HD
    qshaped = query.reshape(seq, heads, HD)
    kshaped = keys.reshape(seq, heads, HD)
    vshaped = values.reshape(seq, heads, HD)
    scores = jnp.einsum("qhd,khd->hqk", qshaped, kshaped, preferred_element_type=jnp.float32)
    scores = scores * (1.0 / math.sqrt(HD))
    rows_idx = lax.broadcasted_iota(jnp.int32, (seq, seq), 0)
    cols_idx = lax.broadcasted_iota(jnp.int32, (seq, seq), 1)
    scores = jnp.where((rows_idx >= cols_idx)[None], scores, -1e30)
    highest = jnp.max(scores, axis=-1, keepdims=True)
    expo = jnp.exp(scores - highest)
    prob = (expo / jnp.sum(expo, axis=-1, keepdims=True)).astype(jnp.bfloat16)
    output = jnp.einsum("hqk,khd->qhd", prob, vshaped, preferred_element_type=jnp.float32)
    return output.astype(jnp.bfloat16).reshape(seq, width)


def scale_rows(stream, mean, spread, gain):
    return ((stream - mean) * lax.rsqrt(spread + 1e-05) * gain[None, :]).astype(jnp.bfloat16)


def per_device(q_seq, k_seq, v_seq, resid, ln_gain, w_up):
    attended = attention_block(q_seq, k_seq, v_seq)
    returned, res_tokens = (
        lax.all_to_all(attended, "col", split_axis=0, concat_axis=1, tiled=True),
        lax.all_to_all(resid, "col", split_axis=0, concat_axis=1, tiled=True),
    )
    stream = res_tokens.astype(jnp.float32) + returned.astype(jnp.float32)
    full_width = stream.shape[1]
    mean = jnp.sum(stream, axis=1, keepdims=True) / full_width
    spread = jnp.sum(stream * stream, axis=1, keepdims=True) / full_width - mean * mean
    normed_tokens = scale_rows(stream, mean, spread, ln_gain)
    normed = lax.all_to_all(normed_tokens, "col", split_axis=1, concat_axis=0, tiled=True)
    whole = lax.all_gather(normed, "col", axis=1, tiled=True)
    product = jnp.dot(
        whole, lax.all_gather(w_up, "row", axis=0, tiled=True), preferred_element_type=jnp.float32
    )
    return jax.nn.gelu(product, approximate=True).astype(jnp.bfloat16)


def solution(mesh):
    placed = (
        P("row", "col"),
        P("row", "col"),
        P("row", "col"),
        P("row", "col"),
        P(),
        P("row", "col"),
    )
    return jax.shard_map(
        per_device, mesh=mesh, in_specs=placed, out_specs=P("row", "col"), check_vma=False
    )
```

profile of v0, /device:TPU:1, one launch (start us, length us, event | category | flops | bytes accessed | tf_op | source)
XLA Modules:
  0.0 229.7 jit_solution(653046495785371151)
XLA Ops:
  6.5 0.0 copy-start
  6.5 10.1 %all-to-all-start = ((bf16[16,8,384]{2,1,0:T(8,128)(2,1)}), bf16[16,8,384]{2,1,0:T(8,128)(2,1)S(1)}, u32[]{:S(2)}, u32[]{:S(2)}) async-start(bf16[16,8,384]{2,1,0:T(8,128)(2,1)} %bitcast.21), calls=%async_computation | async-start | bytes 196608 | tf_op jit(solution)/shard_map/all_to_all | solution.py:36
  16.7 1.0 copy.11
  17.7 1.0 copy.12
  18.7 0.2 fusion.2
  18.9 0.1 fusion.17
  19.0 1.0 copy.15
  20.0 0.3 fusion.4
  20.3 0.1 copy.18
  20.4 0.7 all_to_all.34
  21.1 4.0 %all-to-all-done = bf16[16,8,384]{2,1,0:T(8,128)(2,1)S(1)} async-done(((bf16[16,8,384]{2,1,0:T(8,128)(2,1)}), bf16[16,8,384]{2,1,0:T(8,128)(2,1)S(1)}, u32[]{:S(2)}, u32[]{:S(2)}) %all-to-all-start) | async-done | bytes 98336 | tf_op jit(solution)/shard_map/all_to_all | solution.py:36
  25.1 3.4 %all-to-all-start.1 = ((bf16[16,8,384]{2,1,0:T(8,128)(2,1)}), bf16[16,8,384]{2,1,0:T(8,128)(2,1)S(1)}, u32[]{:S(2)}, u32[]{:S(2)}) async-start(bf16[16,8,384]{2,1,0:T(8,128)(2,1)} %all_to_all.34), calls=%async_computation.1 | async-start | bytes 196608 | tf_op jit(solution)/shard_map/all_to_all | solution.py:35
  28.6 0.0 all-gather.3.cloned.1.call-start
  28.6 0.0 copy-done
  28.6 8.3 %all-to-all-done.1 = bf16[16,8,384]{2,1,0:T(8,128)(2,1)S(1)} async-done(((bf16[16,8,384]{2,1,0:T(8,128)(2,1)}), bf16[16,8,384]{2,1,0:T(8,128)(2,1)S(1)}, u32[]{:S(2)}, u32[]{:S(2)}) %all-to-all-start.1) | async-done | bytes 98336 | tf_op jit(solution)/shard_map/all_to_all | solution.py:35
  36.9 0.2 fusion.13
  37.1 0.1 fusion.14
  37.2 11.6 %all_to_all.42 = bf16[8,16,384]{2,0,1:T(8,128)(2,1)} all-to-all(bf16[8,16,384]{2,0,1:T(8,128)(2,1)S(1)} %fusion.14), channel_id=1, replica_groups=mesh['row'=16,'col'=16] {'col'}, dimensions={1} | all-to-all | bytes 196608 | tf_op jit(solution)/shard_map/all_to_all | solution.py:43
  48.8 0.0 all-gather.3.cloned.1.call-update
  48.8 0.0 all-gather.5.cloned.1.call-start
  48.9 0.7 all-gather.5.cloned.1.call-update
  49.6 35.2 %all-gather.3.cloned.1.call-done = bf16[128,6144]{1,0:T(8,128)(2,1)} async-done(((bf16[128,384]{1,0:T(8,128)(2,1)}), bf16[128,6144]{1,0:T(8,128)(2,1)}) %all-gather.3.cloned.1.call-update) | async-done | bytes 1572880 | tf_op jit(solution)/shard_map/all_gather | solution.py:44
  84.8 127.7 %all-gather.5.cloned.1.call-done = bf16[6144,1536]{1,0:T(8,128)(2,1)} async-done(((bf16[384,1536]{1,0:T(8,128)(2,1)}), bf16[6144,1536]{1,0:T(8,128)(2,1)}) %all-gather.5.cloned.1.call-update) | async-done | bytes 18874384 | tf_op jit(solution)/shard_map/all_gather | solution.py:46
  212.5 10.4 %fusion.12 = bf16[128,1536]{1,0:T(8,128)(2,1)} fusion(bf16[128,6144]{1,0:T(8,128)(2,1)} %all-gather.3.cloned.1.call-done, bf16[6144,1536]{1,0:T(8,128)(2,1)} %all-gather.5.cloned.1.call-done), kind=kOutput, calls=%fused_computation.15 | convolution fusion | flops 2417688576 | bytes 20840448 | tf_op jit(solution)/shard_map/dot_general | solution.py:45
  (3 shorter events, 0.0 us)
Async XLA Ops:
  6.5 22.1 %copy-start = (f32[6144]{0:T(1024)S(1)}, f32[6144]{0:T(1024)}, u32[]{:S(2)}) copy-start(f32[6144]{0:T(1024)} %param.10) | copy-start | bytes 73732
  6.5 18.6 %all-to-all-start = ((bf16[16,8,384]{2,1,0:T(8,128)(2,1)}), bf16[16,8,384]{2,1,0:T(8,128)(2,1)S(1)}, u32[]{:S(2)}, u32[]{:S(2)}) async-start(bf16[16,8,384]{2,1,0:T(8,128)(2,1)} %bitcast.21), calls=%async_computation | async-start | bytes 196608 | tf_op jit(solution)/shard_map/all_to_all | solution.py:36
  25.1 11.8 %all-to-all-start.1 = ((bf16[16,8,384]{2,1,0:T(8,128)(2,1)}), bf16[16,8,384]{2,1,0:T(8,128)(2,1)S(1)}, u32[]{:S(2)}, u32[]{:S(2)}) async-start(bf16[16,8,384]{2,1,0:T(8,128)(2,1)} %all_to_all.34), calls=%async_computation.1 | async-start | bytes 196608 | tf_op jit(solution)/shard_map/all_to_all | solution.py:35
  28.6 56.2 %all-gather.3.cloned.1.call-start = ((), (), s32[]{:S(2)}) async-start(), calls=%async_computation.3 | async-start | bytes 1671168 | tf_op jit(solution)/shard_map/all_gather | solution.py:44
  48.8 163.7 %all-gather.5.cloned.1.call-start = ((), (), s32[]{:S(2)}) async-start(), calls=%async_computation.4 | async-start | bytes 20054016 | tf_op jit(solution)/shard_map/all_gather | solution.py:46
Sparse Core Ops, SparseCore 0:
  48.9 35.7 all-gather.2
  87.2 125.2 all-gather.4
where the time goes:
time: 230 us
  waiting for transfers between devices  176 us (77%)
  starting transfers between devices  13.6 us (6%)
  between operations  13.5 us (6%)
  blocking collectives  11.6 us (5%)
  matrix products  10.9 us (5%)
  local copies, waits for them, and re-layouts  3.85 us (2%)
    all_gather x1, waiting for transfers between devices, per_device(): lax.all_gather(w_up, 'row', axis=0, tiled=True)  128 us
    all_gather x1, waiting for transfers between devices, per_device(): whole = lax.all_gather(normed, 'col', axis=1, tiled=True)  35.2 us
    all_to_all x1, blocking collectives, per_device(): lax.all_to_all(normed_tokens, 'col', split_axis=1, concat_axis=0, tiled=T...  11.6 us
    dot_general x1, matrix products, per_device(): jnp.dot(whole, lax.all_gather(w_up, 'row', axis=0, tiled=True), preferred...  10.4 us
    all_to_all x1, starting transfers between devices, per_device(): lax.all_to_all(resid, 'col', split_axis=0, concat_axis=1, tiled=True)  10.1 us
    all_to_all x1, waiting for transfers between devices, per_device(): lax.all_to_all(attended, 'col', split_axis=0, concat_axis=1, tiled=True)  8.27 us
  transfers between devices with their start and end apart: 4, of which 4 were waited for; matrix products, arithmetic and copies ran while one was open for 2% of the time, Pallas kernels for 0%

commit v1 on v0

--- a/solution.py
+++ b/solution.py
@@ -41,7 +41,14 @@
     spread = jnp.sum(stream * stream, axis=1, keepdims=True) / full_width - mean * mean
     normed_tokens = scale_rows(stream, mean, spread, ln_gain)
     normed = lax.all_to_all(normed_tokens, "col", split_axis=1, concat_axis=0, tiled=True)
-    whole = lax.all_gather(normed, "col", axis=1, tiled=True)
+    size = lax.axis_size("col")
+    forward = [(i, (i + 1) % size) for i in range(size)]
+    terms = [normed]
+    for hop in range(1, size):
+        terms = [lax.ppermute(terms[0], "col", forward), *terms]
+    full = jnp.concatenate(terms, axis=1)
+    shift = (lax.axis_index("col") + 1) * terms[-1].shape[1]
+    whole = jnp.roll(full, shift, axis=1)
     product = jnp.dot(
         whole, lax.all_gather(w_up, "row", axis=0, tiled=True), preferred_element_type=jnp.float32
     )

time: 230 us -> 166 us (0.72)
  the two profiles are of different devices: /device:TPU:1 before, /device:TPU:14 now
where the time goes in v1:
time: 166 us
  waiting for transfers between devices  86.6 us (52%)
  blocking collectives  27.5 us (17%)
  local copies, waits for them, and re-layouts  22.5 us (14%)
  between operations  13.8 us (8%)
  matrix products  10.6 us (6%)
  starting transfers between devices  4.12 us (2%)
    ppermute x15, waiting for transfers between devices, per_device(): terms = [lax.ppermute(terms[0], 'col', forward), *terms]  77.6 us
    unnamed x80, local copies, waits for them, and re-layouts  22.3 us
    all_to_all x1, blocking collectives, per_device(): lax.all_to_all(attended, 'col', split_axis=0, concat_axis=1, tiled=True)  16.7 us
    all_to_all x1, blocking collectives, per_device(): lax.all_to_all(normed_tokens, 'col', split_axis=1, concat_axis=0, tiled=T...  10.9 us
    dot_general x1, matrix products, per_device(): jnp.dot(whole, lax.all_gather(w_up, 'row', axis=0, tiled=True), preferred...  10.1 us
    all_to_all x1, waiting for transfers between devices, per_device(): lax.all_to_all(resid, 'col', split_axis=0, concat_axis=1, tiled=True)  8.25 us
    all_to_all x1, starting transfers between devices, per_device(): lax.all_to_all(resid, 'col', split_axis=0, concat_axis=1, tiled=True)  3.51 us
  transfers between devices with their start and end apart: 17, of which 16 were waited for; matrix products, arithmetic and copies ran while one was open for 10% of the time, Pallas kernels for 0%

profile of v1, /device:TPU:14, one launch (start us, length us, event | category | flops | bytes accessed | tf_op | source)
XLA Modules:
  0.0 165.5 jit_solution(12327807186033235035)
XLA Ops:
  7.3 1.0 copy.11
  8.3 1.0 copy.12
  9.3 1.0 copy.15
  11.1 16.7 %all_to_all.42 = bf16[16,8,384]{2,1,0:T(8,128)(2,1)S(1)} all-to-all(bf16[16,8,384]{2,1,0:T(8,128)(2,1)S(1)} %all_to_all.34), channel_id=1, replica_groups=mesh['row'=16,'col'=16] {'col'}, dimensions={0} | all-to-all | bytes 196608 | tf_op jit(solution)/shard_map/all_to_all | solution.py:35
  27.8 3.5 %all-to-all-start = ((bf16[16,8,384]{2,1,0:T(8,128)(2,1)}), bf16[16,8,384]{2,1,0:T(8,128)(2,1)S(1)}, u32[]{:S(2)}, u32[]{:S(2)}) async-start(bf16[16,8,384]{2,1,0:T(8,128)(2,1)} %bitcast), calls=%async_computation | async-start | bytes 196608 | tf_op jit(solution)/shard_map/all_to_all | solution.py:36
  31.3 8.3 %all-to-all-done = bf16[16,8,384]{2,1,0:T(8,128)(2,1)S(1)} async-done(((bf16[16,8,384]{2,1,0:T(8,128)(2,1)}), bf16[16,8,384]{2,1,0:T(8,128)(2,1)S(1)}, u32[]{:S(2)}, u32[]{:S(2)}) %all-to-all-start) | async-done | bytes 98336 | tf_op jit(solution)/shard_map/all_to_all | solution.py:36
  39.9 10.9 %all_to_all.43 = bf16[8,16,384]{2,0,1:T(8,128)(2,1)S(1)} all-to-all(bf16[8,16,384]{2,0,1:T(8,128)(2,1)S(1)} %fusion.20), channel_id=1, replica_groups=mesh['row'=16,'col'=16] {'col'}, dimensions={1} | all-to-all | bytes 196608 | tf_op jit(solution)/shard_map/all_to_all | solution.py:43
  51.3 4.7 %collective-permute-done = bf16[128,384]{1,0:T(8,128)(2,1)S(1)} collective-permute-done((bf16[128,384]{1,0:T(8,128)(2,1)S(1)}, bf16[128,384]{1,0:T(8,128)(2,1)S(1)}, u32[]{:S(2)}, u32[]{:S(2)}) %collective-permute-start) | collective-permute-done | bytes 98336 | tf_op jit(solution)/shard_map/ppermute | solution.py:48
  56.0 5.2 %collective-permute-done.1 = bf16[128,384]{1,0:T(8,128)(2,1)S(1)} collective-permute-done((bf16[128,384]{1,0:T(8,128)(2,1)S(1)}, bf16[128,384]{1,0:T(8,128)(2,1)S(1)}, u32[]{:S(2)}, u32[]{:S(2)}) %collective-permute-start.1) | collective-permute-done | bytes 98336 | tf_op jit(solution)/shard_map/ppermute | solution.py:48
  61.3 5.2 %collective-permute-done.2 = bf16[128,384]{1,0:T(8,128)(2,1)S(1)} collective-permute-done((bf16[128,384]{1,0:T(8,128)(2,1)S(1)}, bf16[128,384]{1,0:T(8,128)(2,1)S(1)}, u32[]{:S(2)}, u32[]{:S(2)}) %collective-permute-start.2) | collective-permute-done | bytes 98336 | tf_op jit(solution)/shard_map/ppermute | solution.py:48
  66.5 5.2 %collective-permute-done.3 = bf16[128,384]{1,0:T(8,128)(2,1)S(1)} collective-permute-done((bf16[128,384]{1,0:T(8,128)(2,1)S(1)}, bf16[128,384]{1,0:T(8,128)(2,1)S(1)}, u32[]{:S(2)}, u32[]{:S(2)}) %collective-permute-start.3) | collective-permute-done | bytes 98336 | tf_op jit(solution)/shard_map/ppermute | solution.py:48
  72.4 5.2 %collective-permute-done.4 = bf16[128,384]{1,0:T(8,128)(2,1)S(1)} collective-permute-done((bf16[128,384]{1,0:T(8,128)(2,1)S(1)}, bf16[128,384]{1,0:T(8,128)(2,1)S(1)}, u32[]{:S(2)}, u32[]{:S(2)}) %collective-permute-start.4) | collective-permute-done | bytes 98336 | tf_op jit(solution)/shard_map/ppermute | solution.py:48
  78.3 5.2 %collective-permute-done.5 = bf16[128,384]{1,0:T(8,128)(2,1)S(1)} collective-permute-done((bf16[128,384]{1,0:T(8,128)(2,1)S(1)}, bf16[128,384]{1,0:T(8,128)(2,1)S(1)}, u32[]{:S(2)}, u32[]{:S(2)}) %collective-permute-start.5) | collective-permute-done | bytes 98336 | tf_op jit(solution)/shard_map/ppermute | solution.py:48
  84.2 5.2 %collective-permute-done.6 = bf16[128,384]{1,0:T(8,128)(2,1)S(1)} collective-permute-done((bf16[128,384]{1,0:T(8,128)(2,1)S(1)}, bf16[128,384]{1,0:T(8,128)(2,1)S(1)}, u32[]{:S(2)}, u32[]{:S(2)}) %collective-permute-start.6) | collective-permute-done | bytes 98336 | tf_op jit(solution)/shard_map/ppermute | solution.py:48
  90.1 5.2 %collective-permute-done.7 = bf16[128,384]{1,0:T(8,128)(2,1)S(1)} collective-permute-done((bf16[128,384]{1,0:T(8,128)(2,1)S(1)}, bf16[128,384]{1,0:T(8,128)(2,1)S(1)}, u32[]{:S(2)}, u32[]{:S(2)}) %collective-permute-start.7) | collective-permute-done | bytes 98336 | tf_op jit(solution)/shard_map/ppermute | solution.py:48
  96.0 5.2 %collective-permute-done.8 = bf16[128,384]{1,0:T(8,128)(2,1)S(1)} collective-permute-done((bf16[128,384]{1,0:T(8,128)(2,1)S(1)}, bf16[128,384]{1,0:T(8,128)(2,1)S(1)}, u32[]{:S(2)}, u32[]{:S(2)}) %collective-permute-start.8) | collective-permute-done | bytes 98336 | tf_op jit(solution)/shard_map/ppermute | solution.py:48
  101.9 5.2 %collective-permute-done.9 = bf16[128,384]{1,0:T(8,128)(2,1)S(1)} collective-permute-done((bf16[128,384]{1,0:T(8,128)(2,1)S(1)}, bf16[128,384]{1,0:T(8,128)(2,1)S(1)}, u32[]{:S(2)}, u32[]{:S(2)}) %collective-permute-start.9) | collective-permute-done | bytes 98336 | tf_op jit(solution)/shard_map/ppermute | solution.py:48
  107.7 5.2 %collective-permute-done.10 = bf16[128,384]{1,0:T(8,128)(2,1)S(1)} collective-permute-done((bf16[128,384]{1,0:T(8,128)(2,1)S(1)}, bf16[128,384]{1,0:T(8,128)(2,1)S(1)}, u32[]{:S(2)}, u32[]{:S(2)}) %collective-permute-start.10) | collective-permute-done | bytes 98336 | tf_op jit(solution)/shard_map/ppermute | solution.py:48
  113.6 5.2 %collective-permute-done.11 = bf16[128,384]{1,0:T(8,128)(2,1)S(1)} collective-permute-done((bf16[128,384]{1,0:T(8,128)(2,1)S(1)}, bf16[128,384]{1,0:T(8,128)(2,1)S(1)}, u32[]{:S(2)}, u32[]{:S(2)}) %collective-permute-start.11) | collective-permute-done | bytes 98336 | tf_op jit(solution)/shard_map/ppermute | solution.py:48
  119.5 5.2 %collective-permute-done.12 = bf16[128,384]{1,0:T(8,128)(2,1)S(1)} collective-permute-done((bf16[128,384]{1,0:T(8,128)(2,1)S(1)}, bf16[128,384]{1,0:T(8,128)(2,1)S(1)}, u32[]{:S(2)}, u32[]{:S(2)}) %collective-permute-start.12) | collective-permute-done | bytes 98336 | tf_op jit(solution)/shard_map/ppermute | solution.py:48
  125.4 5.2 %collective-permute-done.13 = bf16[128,384]{1,0:T(8,128)(2,1)S(1)} collective-permute-done((bf16[128,384]{1,0:T(8,128)(2,1)S(1)}, bf16[128,384]{1,0:T(8,128)(2,1)S(1)}, u32[]{:S(2)}, u32[]{:S(2)}) %collective-permute-start.13) | collective-permute-done | bytes 98336 | tf_op jit(solution)/shard_map/ppermute | solution.py:48
  131.4 4.6 %collective-permute-done.14 = bf16[128,384]{1,0:T(8,128)(2,1)} collective-permute-done((bf16[128,384]{1,0:T(8,128)(2,1)S(1)}, bf16[128,384]{1,0:T(8,128)(2,1)}, u32[]{:S(2)}, u32[]{:S(2)}) %collective-permute-start.14) | collective-permute-done | bytes 98336 | tf_op jit(solution)/shard_map/ppermute | solution.py:48
  136.0 0.9 constant_dynamic-update-slice_fusion.31
  148.6 10.1 %fusion.16 = bf16[128,1536]{1,0:T(8,128)(2,1)} fusion(bf16[6144,1536]{1,0:T(8,128)(2,1)} %all-gather.2.cloned.1.call-done, bf16[128,12288]{1,0:T(8,128)(2,1)S(1)} %constant_dynamic-update-slice_fusion, s32[]{:T(128)S(6)} %select_n.19), kind=kOutput, calls=%fused_computation.17 | convolution fusion | flops 2417688576 | bytes 20840452 | tf_op jit(solution)/shard_map/dot_general | solution.py:52
  (105 shorter events, 20.8 us)
Async XLA Ops:
  6.5 24.8 %copy-start.22 = (f32[6144]{0:T(1024)S(1)}, f32[6144]{0:T(1024)}, u32[]{:S(2)}) copy-start(f32[6144]{0:T(1024)} %param.10) | copy-start | bytes 73732
  6.5 142.1 %all-gather.2.cloned.1.call-start = ((), (), s32[]{:S(2)}) async-start(), calls=%async_computation.3 | async-start | bytes 20054016 | tf_op jit(solution)/shard_map/all_gather | solution.py:53
  27.8 11.8 %all-to-all-start = ((bf16[16,8,384]{2,1,0:T(8,128)(2,1)}), bf16[16,8,384]{2,1,0:T(8,128)(2,1)S(1)}, u32[]{:S(2)}, u32[]{:S(2)}) async-start(bf16[16,8,384]{2,1,0:T(8,128)(2,1)} %bitcast), calls=%async_computation | async-start | bytes 196608 | tf_op jit(solution)/shard_map/all_to_all | solution.py:36
  50.7 5.3 %collective-permute-start = (bf16[128,384]{1,0:T(8,128)(2,1)S(1)}, bf16[128,384]{1,0:T(8,128)(2,1)S(1)}, u32[]{:S(2)}, u32[]{:S(2)}) collective-permute-start(bf16[128,384]{1,0:T(8,128)(2,1)S(1)} %bitcast.19), channel_id=1, source_target_pairs={{0,1},{1,2},{2,3},{3,4},{4,5},{5,6},{6,7},{7,8},{8,9},{9,10},{10,1... | collective-permute-start | bytes 294920 | tf_op jit(solution)/shard_map/ppermute | solution.py:48
  56.0 5.3 %collective-permute-start.1 = (bf16[128,384]{1,0:T(8,128)(2,1)S(1)}, bf16[128,384]{1,0:T(8,128)(2,1)S(1)}, u32[]{:S(2)}, u32[]{:S(2)}) collective-permute-start(bf16[128,384]{1,0:T(8,128)(2,1)S(1)} %collective-permute-done), channel_id=1, source_target_pairs={{0,1},{1,2},{2,3},{3,4},{4,5},{5,6},{6,7},{7,8},{8,9},{9,10},{10,1... | collective-permute-start | bytes 294920 | tf_op jit(solution)/shard_map/ppermute | solution.py:48
  61.2 5.3 %collective-permute-start.2 = (bf16[128,384]{1,0:T(8,128)(2,1)S(1)}, bf16[128,384]{1,0:T(8,128)(2,1)S(1)}, u32[]{:S(2)}, u32[]{:S(2)}) collective-permute-start(bf16[128,384]{1,0:T(8,128)(2,1)S(1)} %collective-permute-done.1), channel_id=1, source_target_pairs={{0,1},{1,2},{2,3},{3,4},{4,5},{5,6},{6,7},{7,8},{8,9},{9,10},{10,1... | collective-permute-start | bytes 294920 | tf_op jit(solution)/shard_map/ppermute | solution.py:48
  66.5 5.3 %collective-permute-start.3 = (bf16[128,384]{1,0:T(8,128)(2,1)S(1)}, bf16[128,384]{1,0:T(8,128)(2,1)S(1)}, u32[]{:S(2)}, u32[]{:S(2)}) collective-permute-start(bf16[128,384]{1,0:T(8,128)(2,1)S(1)} %collective-permute-done.2), channel_id=1, source_target_pairs={{0,1},{1,2},{2,3},{3,4},{4,5},{5,6},{6,7},{7,8},{8,9},{9,10},{10,1... | collective-permute-start | bytes 294920 | tf_op jit(solution)/shard_map/ppermute | solution.py:48
  72.4 5.3 %collective-permute-start.4 = (bf16[128,384]{1,0:T(8,128)(2,1)S(1)}, bf16[128,384]{1,0:T(8,128)(2,1)S(1)}, u32[]{:S(2)}, u32[]{:S(2)}) collective-permute-start(bf16[128,384]{1,0:T(8,128)(2,1)S(1)} %collective-permute-done.3), channel_id=1, source_target_pairs={{0,1},{1,2},{2,3},{3,4},{4,5},{5,6},{6,7},{7,8},{8,9},{9,10},{10,1... | collective-permute-start | bytes 294920 | tf_op jit(solution)/shard_map/ppermute | solution.py:48
  78.3 5.3 %collective-permute-start.5 = (bf16[128,384]{1,0:T(8,128)(2,1)S(1)}, bf16[128,384]{1,0:T(8,128)(2,1)S(1)}, u32[]{:S(2)}, u32[]{:S(2)}) collective-permute-start(bf16[128,384]{1,0:T(8,128)(2,1)S(1)} %collective-permute-done.4), channel_id=1, source_target_pairs={{0,1},{1,2},{2,3},{3,4},{4,5},{5,6},{6,7},{7,8},{8,9},{9,10},{10,1... | collective-permute-start | bytes 294920 | tf_op jit(solution)/shard_map/ppermute | solution.py:48
  84.2 5.3 %collective-permute-start.6 = (bf16[128,384]{1,0:T(8,128)(2,1)S(1)}, bf16[128,384]{1,0:T(8,128)(2,1)S(1)}, u32[]{:S(2)}, u32[]{:S(2)}) collective-permute-start(bf16[128,384]{1,0:T(8,128)(2,1)S(1)} %collective-permute-done.5), channel_id=1, source_target_pairs={{0,1},{1,2},{2,3},{3,4},{4,5},{5,6},{6,7},{7,8},{8,9},{9,10},{10,1... | collective-permute-start | bytes 294920 | tf_op jit(solution)/shard_map/ppermute | solution.py:48
  90.1 5.3 %collective-permute-start.7 = (bf16[128,384]{1,0:T(8,128)(2,1)S(1)}, bf16[128,384]{1,0:T(8,128)(2,1)S(1)}, u32[]{:S(2)}, u32[]{:S(2)}) collective-permute-start(bf16[128,384]{1,0:T(8,128)(2,1)S(1)} %collective-permute-done.6), channel_id=1, source_target_pairs={{0,1},{1,2},{2,3},{3,4},{4,5},{5,6},{6,7},{7,8},{8,9},{9,10},{10,1... | collective-permute-start | bytes 294920 | tf_op jit(solution)/shard_map/ppermute | solution.py:48
  95.9 5.3 %collective-permute-start.8 = (bf16[128,384]{1,0:T(8,128)(2,1)S(1)}, bf16[128,384]{1,0:T(8,128)(2,1)S(1)}, u32[]{:S(2)}, u32[]{:S(2)}) collective-permute-start(bf16[128,384]{1,0:T(8,128)(2,1)S(1)} %collective-permute-done.7), channel_id=1, source_target_pairs={{0,1},{1,2},{2,3},{3,4},{4,5},{5,6},{6,7},{7,8},{8,9},{9,10},{10,1... | collective-permute-start | bytes 294920 | tf_op jit(solution)/shard_map/ppermute | solution.py:48
  101.8 5.3 %collective-permute-start.9 = (bf16[128,384]{1,0:T(8,128)(2,1)S(1)}, bf16[128,384]{1,0:T(8,128)(2,1)S(1)}, u32[]{:S(2)}, u32[]{:S(2)}) collective-permute-start(bf16[128,384]{1,0:T(8,128)(2,1)S(1)} %collective-permute-done.8), channel_id=1, source_target_pairs={{0,1},{1,2},{2,3},{3,4},{4,5},{5,6},{6,7},{7,8},{8,9},{9,10},{10,1... | collective-permute-start | bytes 294920 | tf_op jit(solution)/shard_map/ppermute | solution.py:48
  107.7 5.3 %collective-permute-start.10 = (bf16[128,384]{1,0:T(8,128)(2,1)S(1)}, bf16[128,384]{1,0:T(8,128)(2,1)S(1)}, u32[]{:S(2)}, u32[]{:S(2)}) collective-permute-start(bf16[128,384]{1,0:T(8,128)(2,1)S(1)} %collective-permute-done.9), channel_id=1, source_target_pairs={{0,1},{1,2},{2,3},{3,4},{4,5},{5,6},{6,7},{7,8},{8,9},{9,10},{10,1... | collective-permute-start | bytes 294920 | tf_op jit(solution)/shard_map/ppermute | solution.py:48
  113.6 5.3 %collective-permute-start.11 = (bf16[128,384]{1,0:T(8,128)(2,1)S(1)}, bf16[128,384]{1,0:T(8,128)(2,1)S(1)}, u32[]{:S(2)}, u32[]{:S(2)}) collective-permute-start(bf16[128,384]{1,0:T(8,128)(2,1)S(1)} %collective-permute-done.10), channel_id=1, source_target_pairs={{0,1},{1,2},{2,3},{3,4},{4,5},{5,6},{6,7},{7,8},{8,9},{9,10},{10,1... | collective-permute-start | bytes 294920 | tf_op jit(solution)/shard_map/ppermute | solution.py:48
  119.5 5.3 %collective-permute-start.12 = (bf16[128,384]{1,0:T(8,128)(2,1)S(1)}, bf16[128,384]{1,0:T(8,128)(2,1)S(1)}, u32[]{:S(2)}, u32[]{:S(2)}) collective-permute-start(bf16[128,384]{1,0:T(8,128)(2,1)S(1)} %collective-permute-done.11), channel_id=1, source_target_pairs={{0,1},{1,2},{2,3},{3,4},{4,5},{5,6},{6,7},{7,8},{8,9},{9,10},{10,1... | collective-permute-start | bytes 294920 | tf_op jit(solution)/shard_map/ppermute | solution.py:48
  125.4 5.3 %collective-permute-start.13 = (bf16[128,384]{1,0:T(8,128)(2,1)S(1)}, bf16[128,384]{1,0:T(8,128)(2,1)S(1)}, u32[]{:S(2)}, u32[]{:S(2)}) collective-permute-start(bf16[128,384]{1,0:T(8,128)(2,1)S(1)} %collective-permute-done.12), channel_id=1, source_target_pairs={{0,1},{1,2},{2,3},{3,4},{4,5},{5,6},{6,7},{7,8},{8,9},{9,10},{10,1... | collective-permute-start | bytes 294920 | tf_op jit(solution)/shard_map/ppermute | solution.py:48
  130.7 5.4 %collective-permute-start.14 = (bf16[128,384]{1,0:T(8,128)(2,1)S(1)}, bf16[128,384]{1,0:T(8,128)(2,1)}, u32[]{:S(2)}, u32[]{:S(2)}) collective-permute-start(bf16[128,384]{1,0:T(8,128)(2,1)S(1)} %collective-permute-done.13), channel_id=1, source_target_pairs={{0,1},{1,2},{2,3},{3,4},{4,5},{5,6},{6,7},{7,8},{8,9},{9,10},{10,1... | collective-permute-start | bytes 294920 | tf_op jit(solution)/shard_map/ppermute | solution.py:48
  131.3 16.9 %copy-start.11 = (bf16[128,384]{1,0:T(8,128)(2,1)S(1)}, bf16[128,384]{1,0:T(8,128)(2,1)}, u32[]{:S(2)}) copy-start(bf16[128,384]{1,0:T(8,128)(2,1)} %copy-done.10) | copy-start | bytes 294916
  131.3 17.0 %copy-start.9 = (bf16[128,384]{1,0:T(8,128)(2,1)S(1)}, bf16[128,384]{1,0:T(8,128)(2,1)}, u32[]{:S(2)}) copy-start(bf16[128,384]{1,0:T(8,128)(2,1)} %copy-done.8) | copy-start | bytes 294916
  131.3 17.0 %copy-start.7 = (bf16[128,384]{1,0:T(8,128)(2,1)S(1)}, bf16[128,384]{1,0:T(8,128)(2,1)}, u32[]{:S(2)}) copy-start(bf16[128,384]{1,0:T(8,128)(2,1)} %copy-done.6) | copy-start | bytes 294916
  131.4 17.0 %copy-start.5 = (bf16[128,384]{1,0:T(8,128)(2,1)S(1)}, bf16[128,384]{1,0:T(8,128)(2,1)}, u32[]{:S(2)}) copy-start(bf16[128,384]{1,0:T(8,128)(2,1)} %copy-done.4) | copy-start | bytes 294916
  131.4 17.0 %copy-start.3 = (bf16[128,384]{1,0:T(8,128)(2,1)S(1)}, bf16[128,384]{1,0:T(8,128)(2,1)}, u32[]{:S(2)}) copy-start(bf16[128,384]{1,0:T(8,128)(2,1)} %copy-done.2) | copy-start | bytes 294916
  131.4 17.1 %copy-start.1 = (bf16[128,384]{1,0:T(8,128)(2,1)S(1)}, bf16[128,384]{1,0:T(8,128)(2,1)}, u32[]{:S(2)}) copy-start(bf16[128,384]{1,0:T(8,128)(2,1)} %copy-done) | copy-start | bytes 294916
  (16 other events, 86.4 us)
Sparse Core Ops, SparseCore 0:
  9.8 128.6 all-gather.1
